TPU v7x, 256 devices: a whole 4x4x8 slice. The times are simulated.
256 devices in a mesh: tm: 32 (over y, z_hi, core), rows: 8 (over z_lo, x).
Axes of the slice: x: 4, y: 4, z: 8 (z_hi: 4, z_lo: 2; z = z_hi * 2 + z_lo), core: 2. Of those that a mesh axis runs over, the one named last changes fastest.
Arguments:
- latent: bfloat16 [32, 16, 128, 512], P('tm', 'rows'), may hold values from -32 to 32
- norm_gain: float32 [512], replicated, may hold values from 0.1 to 1.9
- conv_weight: bfloat16 [27, 512, 512], P(None, 'tm'), may hold values from -0.0546875 to 0.0546875
- grad_out: bfloat16 [32, 16, 128, 512], P('tm', 'rows'), may hold values from -6 to 6
Outputs:
- refined: bfloat16 [32, 16, 128, 512], P('tm', 'rows')
- grad_latent: float32 [32, 16, 128, 512], P('tm', 'rows')
All inputs are finite; a program needn't handle non-finite values.
Results may differ from a plain program's by a relative error of at most 0.0013.
The roundings to bfloat16 on the way count: a program that leaves them out, or rounds other values in their place, can miss the bound.
Values may be sent and summed in bfloat16 or wider, within the bound.
No kernel may reach another device: no remote copies, remote signals or barrier semaphores. Data moves between devices by JAX's collectives and lax.ppermute only.
A program may use at most 64 MiB of HBM per device.

v0:
```python
import jax
import jax.numpy as jnp
from jax import lax
from jax.sharding import PartitionSpec as P

GROUPS = 32


epsilon = 1e-06


def shifted(block, axis, distance):
    devices = range(lax.axis_size(axis))
    route = [(i - distance, i) for i in devices if i - distance in devices]
    return lax.ppermute(block, axis, route)


def with_halo(shard, sides, width):
    for axis, dim in sides:
        size, length = (lax.axis_size(axis), shard.shape[dim])
        up = [(i, (i + 1) % size) for i in range(size - 1)]
        down = [(j, i) for i, j in up]
        last = lax.slice_in_dim(shard, length - width, length, axis=dim)
        first = lax.slice_in_dim(shard, 0, width, axis=dim)
        before = lax.ppermute(last, axis, up)
        after = lax.ppermute(first, axis, down)
        shard = jnp.concatenate([before, shard, after], axis=dim)
    return shard


def grouped_view(values):
    return values.reshape(
        values.shape[0], values.shape[1] * values.shape[2], GROUPS, values.shape[3] // GROUPS
    )


def widen_columns(values):
    return jnp.pad(values, ((0, 0), (0, 0), (1, 1), (0, 0)))


def shards(latent, norm_gain, conv_weight, grad_out):
    frames_here, rows_here, columns, channels = latent.shape
    cell_count = lax.axis_size("rows") * rows_here * columns * (channels // GROUPS)
    full_weight = lax.all_gather(conv_weight, "tm", axis=1, tiled=True)
    latent_wide = latent.astype(jnp.float32)
    grouped = grouped_view(latent_wide)
    average = lax.psum(jnp.sum(grouped, axis=(1, 3)), "rows") / cell_count
    centred = grouped - average[:, None, :, None]
    spread = lax.psum(jnp.sum(centred * centred, axis=(1, 3)), "rows") / cell_count
    inverse = lax.rsqrt(spread + epsilon)
    normed_grouped = centred * inverse[:, None, :, None]
    normed = normed_grouped.reshape(latent.shape)
    scaled = normed * norm_gain
    sigmoid_value = jax.nn.sigmoid(scaled)
    activated = (scaled * sigmoid_value).astype(jnp.bfloat16)
    before_one = shifted(activated, "tm", 1)
    before_two = shifted(activated, "tm", 2)
    padded = with_halo(
        jnp.concatenate([before_two, before_one, activated], axis=0), (("rows", 1),), 1
    )
    after_one = shifted(grad_out, "tm", -1)
    after_two = shifted(grad_out, "tm", -2)
    padded_grad = with_halo(
        jnp.concatenate([grad_out, after_one, after_two], axis=0), (("rows", 1),), 1
    )
    padded = widen_columns(padded)
    padded_grad = widen_columns(padded_grad)
    conv_sum = jnp.zeros((frames_here * rows_here * columns, channels), jnp.float32)
    grad_act = jnp.zeros((frames_here * rows_here * columns, channels), jnp.float32)
    for time_tap in range(3):
        for row_tap in range(3):
            for col_tap in range(3):
                tap_weight = full_weight[time_tap * 9 + row_tap * 3 + col_tap]
                window = padded[
                    time_tap : time_tap + frames_here,
                    row_tap : row_tap + rows_here,
                    col_tap : col_tap + columns,
                ]
                conv_sum = conv_sum + jnp.dot(
                    window.reshape(-1, channels), tap_weight, preferred_element_type=jnp.float32
                )
                back_window = padded_grad[
                    2 - time_tap : 2 - time_tap + frames_here,
                    2 - row_tap : 2 - row_tap + rows_here,
                    2 - col_tap : 2 - col_tap + columns,
                ]
                grad_act = grad_act + lax.dot_general(
                    back_window.reshape(-1, channels),
                    tap_weight,
                    (((1,), (1,)), ((), ())),
                    preferred_element_type=jnp.float32,
                )
    refined = (latent_wide + conv_sum.reshape(latent.shape)).astype(jnp.bfloat16)
    grad_scaled = (
        grad_act.reshape(latent.shape) * sigmoid_value * (1.0 + scaled * (1.0 - sigmoid_value))
    )
    grad_normed = grouped_view(grad_scaled * norm_gain)
    first_sum, second_sum = lax.psum(
        (jnp.sum(grad_normed, axis=(1, 3)), jnp.sum(grad_normed * normed_grouped, axis=(1, 3))),
        "rows",
    )
    first = first_sum / cell_count
    second = second_sum / cell_count
    grad_norm_part = (
        grad_normed - first[:, None, :, None] - normed_grouped * second[:, None, :, None]
    ) * inverse[:, None, :, None]
    grad_latent = grad_out.astype(jnp.float32) + grad_norm_part.reshape(latent.shape)
    return (refined, grad_latent)


def solution(mesh):
    placed = (P("tm", "rows", None, None), P(), P(None, "tm", None), P("tm", "rows", None, None))
    return jax.shard_map(
        shards,
        mesh=mesh,
        in_specs=placed,
        out_specs=(P("tm", "rows", None, None), P("tm", "rows", None, None)),
        check_vma=False,
    )
```

profile of v0, /device:TPU:6, one launch (start us, length us, event | category | flops | bytes accessed | tf_op | source)
XLA Modules:
  0.0 219.8 jit_solution(12708673439425601817)
XLA Ops:
  7.9 1.3 collective-permute-start.4
  11.7 16.1 %psum.28 = f32[1,32]{1,0:T(1,128)S(1)} all-reduce(f32[1,32]{1,0:T(1,128)S(1)} %bitcast.290), channel_id=1, replica_groups=mesh['tm'=32,'rows'=8] {'rows'}, use_global_device_ids=true, to_apply=%region_2.0 | all-reduce | flops 32 | bytes 256 | tf_op jit(solution)/shard_map/psum | solution.py:47
  28.8 5.3 %collective-permute-done.5 = bf16[1,2,128,512]{3,2,1,0:T(8,128)(2,1)S(1)} collective-permute-done((bf16[1,2,128,512]{3,2,1,0:T(8,128)(2,1)}, bf16[1,2,128,512]{3,2,1,0:T(8,128)(2,1)S(1)}, u32[]{:S(2)}, u32[]{:S(2)}) %collective-permute-start.5) | collective-permute-done | bytes 262176 | tf_op jit(solution)/shard_map/ppermute | solution.py:15
  34.9 1.9 collective-permute-start.6
  36.8 3.9 %collective-permute-start.7 = (bf16[3,1,128,512]{3,2,1,0:T(8,128)(2,1)S(1)}, bf16[3,1,128,512]{3,2,1,0:T(8,128)(2,1)S(1)}, u32[]{:S(2)}, u32[]{:S(2)}) collective-permute-start(bf16[3,1,128,512]{3,2,1,0:T(8,128)(2,1)S(1)} %get-tuple-element.59), channel_id=1, source_target_pairs={{1,0},{2,1},{3,2},{4,3},{5,4},{6,5},{7,6},{9,8},{10,9},{11,10},{12... | collective-permute-start | bytes 1179656 | tf_op jit(solution)/shard_map/ppermute | solution.py:26
  42.1 22.3 %psum.29 = f32[1,32]{1,0:T(1,128)S(1)} all-reduce(f32[1,32]{1,0:T(1,128)S(1)} %bitcast.291), channel_id=1, replica_groups=mesh['tm'=32,'rows'=8] {'rows'}, use_global_device_ids=true, to_apply=%region_5.6 | all-reduce | flops 32 | bytes 256 | tf_op jit(solution)/shard_map/psum | solution.py:49
  66.2 1.7 fusion.87
  67.9 52.9 %all-gather.2.cloned.1.call-done = bf16[27,512,512]{2,1,0:T(8,128)(2,1)} async-done(((bf16[27,16,512]{2,1,0:T(8,128)(2,1)}), bf16[27,512,512]{2,1,0:T(8,128)(2,1)}) %all-gather.2.cloned.1.call-update) | async-done | bytes 14155792 | tf_op jit(solution)/shard_map/all_gather | solution.py:44
  120.8 1.6 fusion.59
  122.4 2.1 fusion.41
  124.6 2.2 fusion.77
  126.7 1.4 fusion.53
  128.2 1.5 fusion.35
  129.7 1.5 fusion.71
  131.1 1.5 fusion.81
  132.6 1.4 fusion.65
  134.0 1.4 fusion.47
  135.5 1.5 fusion.79
  137.0 1.5 fusion.33
  145.7 2.3 %collective-permute-start.1 = (bf16[1,2,128,512]{3,2,1,0:T(8,128)(2,1)S(1)}, bf16[1,2,128,512]{3,2,1,0:T(8,128)(2,1)S(1)}, u32[]{:S(2)}, u32[]{:S(2)}) collective-permute-start(bf16[1,2,128,512]{3,2,1,0:T(8,128)(2,1)S(1)} %get-tuple-element.62), channel_id=1, source_target_pairs={{0,8},{8,16},{16,24},{24,32},{32,40},{40,48},{48,56},{56,64},{64,7... | collective-permute-start | bytes 786440 | tf_op jit(solution)/shard_map/ppermute | solution.py:15
  148.0 6.9 %collective-permute-start = (bf16[1,2,128,512]{3,2,1,0:T(8,128)(2,1)S(1)}, bf16[1,2,128,512]{3,2,1,0:T(8,128)(2,1)S(1)}, u32[]{:S(2)}, u32[]{:S(2)}) collective-permute-start(bf16[1,2,128,512]{3,2,1,0:T(8,128)(2,1)S(1)} %get-tuple-element.62), channel_id=1, source_target_pairs={{0,16},{8,24},{16,32},{24,40},{32,48},{40,56},{48,64},{56,72},{64,... | collective-permute-start | bytes 786440 | tf_op jit(solution)/shard_map/ppermute | solution.py:15
  155.2 22.7 %all-reduce.2 = (f32[1,32]{1,0:T(1,128)S(1)}, f32[1,32]{1,0:T(1,128)S(1)}) all-reduce(f32[1,32]{1,0:T(1,128)S(1)} %bitcast.289, f32[1,32]{1,0:T(1,128)S(1)} %bitcast.288), channel_id=1, replica_groups=mesh['tm'=32,'rows'=8] {'rows'}, use_global_device_ids=true, to_apply=%region_11.12 | all-reduce | flops 64 | bytes 512 | tf_op jit(solution)/shard_map/psum | solution.py:98
  178.3 1.3 fusion.78
  179.8 3.7 %collective-permute-start.2 = (bf16[3,1,128,512]{3,2,1,0:T(8,128)(2,1)S(1)}, bf16[3,1,128,512]{3,2,1,0:T(8,128)(2,1)S(1)}, u32[]{:S(2)}, u32[]{:S(2)}) collective-permute-start(bf16[3,1,128,512]{3,2,1,0:T(8,128)(2,1)S(1)} %get-tuple-element.60), channel_id=1, source_target_pairs={{0,1},{1,2},{2,3},{3,4},{4,5},{5,6},{6,7},{8,9},{9,10},{10,11},{11... | collective-permute-start | bytes 1179656 | tf_op jit(solution)/shard_map/ppermute | solution.py:25
  183.6 2.3 %collective-permute-start.3 = (bf16[3,1,128,512]{3,2,1,0:T(8,128)(2,1)S(1)}, bf16[3,1,128,512]{3,2,1,0:T(8,128)(2,1)S(1)}, u32[]{:S(2)}, u32[]{:S(2)}) collective-permute-start(bf16[3,1,128,512]{3,2,1,0:T(8,128)(2,1)S(1)} %get-tuple-element.61), channel_id=1, source_target_pairs={{1,0},{2,1},{3,2},{4,3},{5,4},{6,5},{7,6},{9,8},{10,9},{11,10},{12... | collective-permute-start | bytes 1179656 | tf_op jit(solution)/shard_map/ppermute | solution.py:26
  185.9 1.5 fusion.42
  187.4 1.3 fusion.60
  188.7 4.1 %collective-permute-done.2 = bf16[3,1,128,512]{3,2,1,0:T(8,128)(2,1)S(1)} collective-permute-done((bf16[3,1,128,512]{3,2,1,0:T(8,128)(2,1)S(1)}, bf16[3,1,128,512]{3,2,1,0:T(8,128)(2,1)S(1)}, u32[]{:S(2)}, u32[]{:S(2)}) %collective-permute-start.2) | collective-permute-done | bytes 393248 | tf_op jit(solution)/shard_map/ppermute | solution.py:25
  192.9 5.6 %collective-permute-done.3 = bf16[3,1,128,512]{3,2,1,0:T(8,128)(2,1)S(1)} collective-permute-done((bf16[3,1,128,512]{3,2,1,0:T(8,128)(2,1)S(1)}, bf16[3,1,128,512]{3,2,1,0:T(8,128)(2,1)S(1)}, u32[]{:S(2)}, u32[]{:S(2)}) %collective-permute-start.3) | collective-permute-done | bytes 393248 | tf_op jit(solution)/shard_map/ppermute | solution.py:26
  200.1 1.8 fusion.66
  202.0 1.3 fusion.48
  203.3 1.3 fusion.82
  (107 shorter events, 25.8 us)
Async XLA Ops:
  7.2 117.4 %copy-start.2 = (bf16[1,2,128,512]{3,2,1,0:T(8,128)(2,1)S(1)}, bf16[1,2,128,512]{3,2,1,0:T(8,128)(2,1)}, u32[]{:S(2)}) copy-start(bf16[1,2,128,512]{3,2,1,0:T(8,128)(2,1)} %param.7) | copy-start | bytes 786436
  7.2 113.7 %all-gather.2.cloned.1.call-start = ((), (), s32[]{:S(2)}) async-start(), calls=%async_computation | async-start | bytes 14598144 | tf_op jit(solution)/shard_map/all_gather | solution.py:44
  7.9 20.9 %collective-permute-start.4 = (bf16[1,2,128,512]{3,2,1,0:T(8,128)(2,1)}, bf16[1,2,128,512]{3,2,1,0:T(8,128)(2,1)S(1)}, u32[]{:S(2)}, u32[]{:S(2)}) collective-permute-start(bf16[1,2,128,512]{3,2,1,0:T(8,128)(2,1)} %param.7), channel_id=1, source_target_pairs={{8,0},{16,8},{24,16},{32,24},{40,32},{48,40},{56,48},{64,56},{72,6... | collective-permute-start | bytes 786440 | tf_op jit(solution)/shard_map/ppermute | solution.py:15
  9.2 24.9 %collective-permute-start.5 = (bf16[1,2,128,512]{3,2,1,0:T(8,128)(2,1)}, bf16[1,2,128,512]{3,2,1,0:T(8,128)(2,1)S(1)}, u32[]{:S(2)}, u32[]{:S(2)}) collective-permute-start(bf16[1,2,128,512]{3,2,1,0:T(8,128)(2,1)} %param.7), channel_id=1, source_target_pairs={{16,0},{24,8},{32,16},{40,24},{48,32},{56,40},{64,48},{72,56},{80,... | collective-permute-start | bytes 786440 | tf_op jit(solution)/shard_map/ppermute | solution.py:15
  28.8 5.5 %copy-start.6 = (bf16[1,2,128,512]{3,2,1,0:T(8,128)(2,1)}, bf16[1,2,128,512]{3,2,1,0:T(8,128)(2,1)S(1)}, u32[]{:S(2)}) copy-start(bf16[1,2,128,512]{3,2,1,0:T(8,128)(2,1)S(1)} %collective-permute-done.4) | copy-start | bytes 786436
  34.2 0.7 copy-start.7
  34.9 29.8 %collective-permute-start.6 = (bf16[3,1,128,512]{3,2,1,0:T(8,128)(2,1)S(1)}, bf16[3,1,128,512]{3,2,1,0:T(8,128)(2,1)S(1)}, u32[]{:S(2)}, u32[]{:S(2)}) collective-permute-start(bf16[3,1,128,512]{3,2,1,0:T(8,128)(2,1)S(1)} %get-tuple-element.58), channel_id=1, source_target_pairs={{0,1},{1,2},{2,3},{3,4},{4,5},{5,6},{6,7},{8,9},{9,10},{10,11},{11... | collective-permute-start | bytes 1179656 | tf_op jit(solution)/shard_map/ppermute | solution.py:25
  36.8 27.9 %collective-permute-start.7 = (bf16[3,1,128,512]{3,2,1,0:T(8,128)(2,1)S(1)}, bf16[3,1,128,512]{3,2,1,0:T(8,128)(2,1)S(1)}, u32[]{:S(2)}, u32[]{:S(2)}) collective-permute-start(bf16[3,1,128,512]{3,2,1,0:T(8,128)(2,1)S(1)} %get-tuple-element.59), channel_id=1, source_target_pairs={{1,0},{2,1},{3,2},{4,3},{5,4},{6,5},{7,6},{9,8},{10,9},{11,10},{12... | collective-permute-start | bytes 1179656 | tf_op jit(solution)/shard_map/ppermute | solution.py:26
  120.8 17.6 %copy-start = (bf16[27,512,512]{2,1,0:T(8,128)(2,1)S(1)}, bf16[27,512,512]{2,1,0:T(8,128)(2,1)}, u32[]{:S(2)}) copy-start(bf16[27,512,512]{2,1,0:T(8,128)(2,1)} %all-gather.2.cloned.1.call-done) | copy-start | bytes 42467332
  120.8 18.9 %copy-start.5 = (bf16[1,2,128,512]{3,2,1,0:T(8,128)(2,1)S(1)}, bf16[1,2,128,512]{3,2,1,0:T(8,128)(2,1)}, u32[]{:S(2)}) copy-start(bf16[1,2,128,512]{3,2,1,0:T(8,128)(2,1)} %get-tuple-element.11) | copy-start | bytes 786436
  120.8 19.2 %copy-start.4 = (bf16[1,2,128,512]{3,2,1,0:T(8,128)(2,1)S(1)}, bf16[1,2,128,512]{3,2,1,0:T(8,128)(2,1)}, u32[]{:S(2)}) copy-start(bf16[1,2,128,512]{3,2,1,0:T(8,128)(2,1)} %get-tuple-element.12) | copy-start | bytes 786436
  120.8 19.6 %copy-start.3 = (bf16[1,2,128,512]{3,2,1,0:T(8,128)(2,1)S(1)}, bf16[1,2,128,512]{3,2,1,0:T(8,128)(2,1)}, u32[]{:S(2)}) copy-start(bf16[1,2,128,512]{3,2,1,0:T(8,128)(2,1)} %get-tuple-element.13) | copy-start | bytes 786436
  141.1 4.2 %copy-start.1 = (bf16[1,2,128,512]{3,2,1,0:T(8,128)(2,1)S(1)}, bf16[1,2,128,512]{3,2,1,0:T(8,128)(2,1)}, u32[]{:S(2)}) copy-start(bf16[1,2,128,512]{3,2,1,0:T(8,128)(2,1)} %param.4) | copy-start | bytes 786436
  141.1 4.2 %copy-start.8 = (f32[512]{0:T(512)S(1)}, f32[512]{0:T(512)}, u32[]{:S(2)}) copy-start(f32[512]{0:T(512)} %param.5) | copy-start | bytes 6148
  145.3 59.3 %slice-start = ((s8[14155776]{0:T(1024)(128)(4,1)}), s8[1572864]{0:T(1024)(128)(4,1)S(1)}, s32[]{:S(2)}) async-start(s8[14155776]{0:T(1024)(128)(4,1)} %bitcast.231), calls=%async_computation.1 | async-start | bytes 3145728
  145.7 34.0 %collective-permute-start.1 = (bf16[1,2,128,512]{3,2,1,0:T(8,128)(2,1)S(1)}, bf16[1,2,128,512]{3,2,1,0:T(8,128)(2,1)S(1)}, u32[]{:S(2)}, u32[]{:S(2)}) collective-permute-start(bf16[1,2,128,512]{3,2,1,0:T(8,128)(2,1)S(1)} %get-tuple-element.62), channel_id=1, source_target_pairs={{0,8},{8,16},{16,24},{24,32},{32,40},{40,48},{48,56},{56,64},{64,7... | collective-permute-start | bytes 786440 | tf_op jit(solution)/shard_map/ppermute | solution.py:15
  148.0 31.7 %collective-permute-start = (bf16[1,2,128,512]{3,2,1,0:T(8,128)(2,1)S(1)}, bf16[1,2,128,512]{3,2,1,0:T(8,128)(2,1)S(1)}, u32[]{:S(2)}, u32[]{:S(2)}) collective-permute-start(bf16[1,2,128,512]{3,2,1,0:T(8,128)(2,1)S(1)} %get-tuple-element.62), channel_id=1, source_target_pairs={{0,16},{8,24},{16,32},{24,40},{32,48},{40,56},{48,64},{56,72},{64,... | collective-permute-start | bytes 786440 | tf_op jit(solution)/shard_map/ppermute | solution.py:15
  179.8 13.0 %collective-permute-start.2 = (bf16[3,1,128,512]{3,2,1,0:T(8,128)(2,1)S(1)}, bf16[3,1,128,512]{3,2,1,0:T(8,128)(2,1)S(1)}, u32[]{:S(2)}, u32[]{:S(2)}) collective-permute-start(bf16[3,1,128,512]{3,2,1,0:T(8,128)(2,1)S(1)} %get-tuple-element.60), channel_id=1, source_target_pairs={{0,1},{1,2},{2,3},{3,4},{4,5},{5,6},{6,7},{8,9},{9,10},{10,11},{11... | collective-permute-start | bytes 1179656 | tf_op jit(solution)/shard_map/ppermute | solution.py:25
  183.6 14.8 %collective-permute-start.3 = (bf16[3,1,128,512]{3,2,1,0:T(8,128)(2,1)S(1)}, bf16[3,1,128,512]{3,2,1,0:T(8,128)(2,1)S(1)}, u32[]{:S(2)}, u32[]{:S(2)}) collective-permute-start(bf16[3,1,128,512]{3,2,1,0:T(8,128)(2,1)S(1)} %get-tuple-element.61), channel_id=1, source_target_pairs={{1,0},{2,1},{3,2},{4,3},{5,4},{6,5},{7,6},{9,8},{10,9},{11,10},{12... | collective-permute-start | bytes 1179656 | tf_op jit(solution)/shard_map/ppermute | solution.py:26
  185.9 18.8 %slice-start.1 = ((s8[14155776]{0:T(1024)(128)(4,1)}), s8[4194304]{0:T(1024)(128)(4,1)S(1)}, s32[]{:S(2)}) async-start(s8[14155776]{0:T(1024)(128)(4,1)} %bitcast.231), calls=%async_computation.2 | async-start | bytes 8388608
  199.2 5.5 %slice-start.2 = ((s8[14155776]{0:T(1024)(128)(4,1)}), s8[4194304]{0:T(1024)(128)(4,1)S(1)}, s32[]{:S(2)}) async-start(s8[14155776]{0:T(1024)(128)(4,1)} %bitcast.231), calls=%async_computation.3 | async-start | bytes 8388608
  199.9 4.7 %slice-start.3 = ((s8[14155776]{0:T(1024)(128)(4,1)}), s8[4194304]{0:T(1024)(128)(4,1)S(1)}, s32[]{:S(2)}) async-start(s8[14155776]{0:T(1024)(128)(4,1)} %bitcast.231), calls=%async_computation.4 | async-start | bytes 8388608
Sparse Core Ops, SparseCore 0:
  10.6 110.1 all-gather.1
where the time goes:
time: 221 us; the launch traced here: 220 us
  waiting for transfers between devices  68.6 us (31%)
  blocking collectives  61.2 us (28%)
  matrix products  39.8 us (18%)
  starting transfers between devices  23.6 us (11%)
  between operations  14.8 us (7%)
  other arithmetic  6.57 us (3%)
  local copies, waits for them, and re-layouts  5.16 us (2%)
    all_gather x1, waiting for transfers between devices, shards(): full_weight = lax.all_gather(conv_weight, 'tm', axis=1, tiled=True)  52.9 us
    dot_general x27, matrix products, shards(): lax.dot_general(back_window.reshape(-1, channels), tap_weight, (((1,), (1...  24.2 us
    psum x1, blocking collectives, shards(): lax.psum((jnp.sum(grad_normed, axis=(1, 3)), jnp.sum(grad_normed * normed...  22.7 us
    psum x1, blocking collectives, shards(): lax.psum(jnp.sum(centred * centred, axis=(1, 3)), 'rows') / cell_count  22.3 us
    psum x1, blocking collectives, shards(): average = lax.psum(jnp.sum(grouped, axis=(1, 3)), 'rows') / cell_count  16.1 us
    dot_general x27, matrix products, shards(): jnp.dot(window.reshape(-1, channels), tap_weight, preferred_element_type=...  15.7 us
    ppermute x4, starting transfers between devices, shifted(): return lax.ppermute(block, axis, route)  11.8 us
    ppermute x2, starting transfers between devices, with_halo(): after = lax.ppermute(first, axis, down)  6.21 us
  transfers between devices with their start and end apart: 9, of which 4 were waited for; matrix products, arithmetic and copies ran while one was open for 5% of the time, Pallas kernels for 0%

commit v1 on v0

--- a/solution.py
+++ b/solution.py
@@ -38,10 +38,29 @@
     return jnp.pad(values, ((0, 0), (0, 0), (1, 1), (0, 0)))
 
 
+def plane_windows(plane, rows_here, columns, flip):
+    taps = []
+    for row_tap in range(3):
+        for col_tap in range(3):
+            r0 = 2 - row_tap if flip else row_tap
+            c0 = 2 - col_tap if flip else col_tap
+            window = plane[r0 : r0 + rows_here, c0 : c0 + columns]
+            taps.append(window.reshape(rows_here * columns, 1, plane.shape[-1]))
+    return jnp.concatenate(taps, axis=1)
+
+
 def shards(latent, norm_gain, conv_weight, grad_out):
     frames_here, rows_here, columns, channels = latent.shape
     cell_count = lax.axis_size("rows") * rows_here * columns * (channels // GROUPS)
-    full_weight = lax.all_gather(conv_weight, "tm", axis=1, tiled=True)
+    weight_parts = [
+        lax.all_gather(conv_weight[9 * a : 9 * a + 9], "tm", axis=1, tiled=True) for a in range(3)
+    ]
+    after_one = shifted(grad_out, "tm", -1)
+    after_two = shifted(grad_out, "tm", -2)
+    padded_grad = with_halo(
+        jnp.concatenate([grad_out, after_one, after_two], axis=0), (("rows", 1),), 1
+    )
+    padded_grad = widen_columns(padded_grad)
     latent_wide = latent.astype(jnp.float32)
     grouped = grouped_view(latent_wide)
     average = lax.psum(jnp.sum(grouped, axis=(1, 3)), "rows") / cell_count
@@ -58,47 +77,39 @@
     padded = with_halo(
         jnp.concatenate([before_two, before_one, activated], axis=0), (("rows", 1),), 1
     )
-    after_one = shifted(grad_out, "tm", -1)
-    after_two = shifted(grad_out, "tm", -2)
-    padded_grad = with_halo(
-        jnp.concatenate([grad_out, after_one, after_two], axis=0), (("rows", 1),), 1
-    )
     padded = widen_columns(padded)
-    padded_grad = widen_columns(padded_grad)
-    conv_sum = jnp.zeros((frames_here * rows_here * columns, channels), jnp.float32)
-    grad_act = jnp.zeros((frames_here * rows_here * columns, channels), jnp.float32)
+    positions = frames_here * rows_here * columns
+    grad_act = None
+    conv_sum = None
     for time_tap in range(3):
-        for row_tap in range(3):
-            for col_tap in range(3):
-                tap_weight = full_weight[time_tap * 9 + row_tap * 3 + col_tap]
-                window = padded[
-                    time_tap : time_tap + frames_here,
-                    row_tap : row_tap + rows_here,
-                    col_tap : col_tap + columns,
-                ]
-                conv_sum = conv_sum + jnp.dot(
-                    window.reshape(-1, channels), tap_weight, preferred_element_type=jnp.float32
-                )
-                back_window = padded_grad[
-                    2 - time_tap : 2 - time_tap + frames_here,
-                    2 - row_tap : 2 - row_tap + rows_here,
-                    2 - col_tap : 2 - col_tap + columns,
-                ]
-                grad_act = grad_act + lax.dot_general(
-                    back_window.reshape(-1, channels),
-                    tap_weight,
-                    (((1,), (1,)), ((), ())),
-                    preferred_element_type=jnp.float32,
-                )
-    refined = (latent_wide + conv_sum.reshape(latent.shape)).astype(jnp.bfloat16)
+        part = weight_parts[time_tap]
+        if time_tap > 0:
+            part, grad_act, conv_sum = lax.optimization_barrier((part, grad_act, conv_sum))
+        back = plane_windows(padded_grad[2 - time_tap], rows_here, columns, True)
+        term = lax.dot_general(
+            back, part, (((1, 2), (0, 2)), ((), ())), preferred_element_type=jnp.float32
+        )
+        grad_act = term if grad_act is None else grad_act + term
+        fwd = plane_windows(padded[time_tap], rows_here, columns, False)
+        term = jnp.dot(
+            fwd.reshape(positions, 9 * channels),
+            part.reshape(9 * channels, channels),
+            preferred_element_type=jnp.float32,
+        )
+        conv_sum = term if conv_sum is None else conv_sum + term
     grad_scaled = (
         grad_act.reshape(latent.shape) * sigmoid_value * (1.0 + scaled * (1.0 - sigmoid_value))
     )
     grad_normed = grouped_view(grad_scaled * norm_gain)
-    first_sum, second_sum = lax.psum(
-        (jnp.sum(grad_normed, axis=(1, 3)), jnp.sum(grad_normed * normed_grouped, axis=(1, 3))),
-        "rows",
+    partial = jnp.stack(
+        [jnp.sum(grad_normed, axis=(1, 3)), jnp.sum(grad_normed * normed_grouped, axis=(1, 3))]
     )
+    size = lax.axis_size("rows")
+    total = partial
+    for distance in range(1, size):
+        total = total + lax.ppermute(partial, "rows", [(i, (i + distance) % size) for i in range(size)])
+    first_sum, second_sum = total
+    refined = (latent_wide + conv_sum.reshape(latent.shape)).astype(jnp.bfloat16)
     first = first_sum / cell_count
     second = second_sum / cell_count
     grad_norm_part = (

time: 221 us -> 248 us (1.12)
  waiting for transfers between devices: 68.6 us -> 122 us
  blocking collectives: 61.2 us -> 33.9 us
  matrix products: 39.8 us -> 22.7 us
  local copies, waits for them, and re-layouts: 5.16 us -> 15.9 us
  starting transfers between devices: 23.6 us -> 30.8 us
    all_gather x1 -> x3, waiting for transfers between devices: 52.9 us -> 84.5 us  [shards(): lax.all_gather(conv_weight[9 * a:9 * a + 9], 'tm', axis=1, tiled=True)]
    psum x1 -> x0, blocking collectives: 22.7 us -> none  [shards(): lax.psum((jnp.sum(grad_normed, axis=(1, 3)), jnp.sum(grad_normed * normed...]
    ppermute x4, waiting for transfers between devices: 5.33 us -> 27.9 us  [shifted(): return lax.ppermute(block, axis, route)]
    dot_general x54 -> x6, matrix products: 39.8 us -> 22.7 us  [the longest x3 14.6 us: shards(): jnp.dot(fwd.reshape(positions, 9 * channels), part.reshape(9 * channels,...]
    ppermute x0 -> x7, starting transfers between devices: none -> 9.77 us  [shards(): lax.ppermute(partial, 'rows', [(i, (i + distance) % size) for i in range(...]
    unnamed x28 -> x74, local copies, waits for them, and re-layouts: 1.62 us -> 9.03 us
    ppermute x2, waiting for transfers between devices: 4.13 us -> 0.01 us  [with_halo(): before = lax.ppermute(last, axis, up)]
    psum x1, blocking collectives: 22.3 us -> 18.2 us  [shards(): lax.psum(jnp.sum(centred * centred, axis=(1, 3)), 'rows') / cell_count]
  transfers between devices with their start and end apart: 9 -> 18, of which waited for: 4 -> 6; matrix products, arithmetic and copies ran while one was open for 5% -> 14% of each run, Pallas kernels for 0% -> 0%
where the time goes in v1:
time: 248 us; the launch traced here: 247 us
  waiting for transfers between devices  122 us (49%)
  blocking collectives  33.9 us (14%)
  starting transfers between devices  30.8 us (12%)
  matrix products  22.7 us (9%)
  local copies, waits for them, and re-layouts  15.9 us (6%)
  between operations  14.4 us (6%)
  other arithmetic  6.37 us (3%)
    all_gather x3, waiting for transfers between devices, shards(): lax.all_gather(conv_weight[9 * a:9 * a + 9], 'tm', axis=1, tiled=True)  84.5 us
    ppermute x4, waiting for transfers between devices, shifted(): return lax.ppermute(block, axis, route)  27.9 us
    psum x1, blocking collectives, shards(): lax.psum(jnp.sum(centred * centred, axis=(1, 3)), 'rows') / cell_count  18.2 us
    psum x1, blocking collectives, shards(): average = lax.psum(jnp.sum(grouped, axis=(1, 3)), 'rows') / cell_count  15.7 us
    dot_general x3, matrix products, shards(): jnp.dot(fwd.reshape(positions, 9 * channels), part.reshape(9 * channels,...  14.6 us
    ppermute x7, starting transfers between devices, shards(): lax.ppermute(partial, 'rows', [(i, (i + distance) % size) for i in range(...  9.77 us
    ppermute x2, waiting for transfers between devices, with_halo(): after = lax.ppermute(first, axis, down)  9.32 us
    ppermute x4, starting transfers between devices, shifted(): return lax.ppermute(block, axis, route)  9.22 us
  transfers between devices with their start and end apart: 18, of which 6 were waited for; matrix products, arithmetic and copies ran while one was open for 14% of the time, Pallas kernels for 0%

profile of v1, /device:TPU:6, one launch (start us, length us, event | category | flops | bytes accessed | tf_op | source)
XLA Modules:
  0.0 246.7 jit_solution(14454695460955300014)
XLA Ops:
  7.2 1.9 fusion.39
  9.9 1.0 convert_reduce_fusion
  11.1 15.7 %psum.14 = f32[1,32]{1,0:T(1,128)S(1)} all-reduce(f32[1,32]{1,0:T(1,128)S(1)} %bitcast.172), channel_id=1, replica_groups=mesh['tm'=32,'rows'=8] {'rows'}, use_global_device_ids=true, to_apply=%region_2.3 | all-reduce | flops 32 | bytes 256 | tf_op jit(solution)/shard_map/psum | solution.py:66
  27.0 1.1 fusion.25
  28.2 18.2 %psum.15 = f32[1,32]{1,0:T(1,128)S(1)} all-reduce(f32[1,32]{1,0:T(1,128)S(1)} %bitcast.173), channel_id=1, replica_groups=mesh['tm'=32,'rows'=8] {'rows'}, use_global_device_ids=true, to_apply=%region_5.6 | all-reduce | flops 32 | bytes 256 | tf_op jit(solution)/shard_map/psum | solution.py:68
  46.6 1.1 fusion.17
  47.8 5.3 %collective-permute-start.4 = (bf16[1,2,128,512]{3,2,1,0:T(8,128)(2,1)S(1)}, bf16[1,2,128,512]{3,2,1,0:T(8,128)(2,1)S(1)}, u32[]{:S(2)}, u32[]{:S(2)}) collective-permute-start(bf16[1,2,128,512]{3,2,1,0:T(8,128)(2,1)S(1)} %fusion.17), channel_id=1, source_target_pairs={{0,16},{8,24},{16,32},{24,40},{32,48},{40,56},{48,64},{56,72},{64,... | collective-permute-start | bytes 786440 | tf_op jit(solution)/shard_map/ppermute | solution.py:15
  53.1 1.3 collective-permute-start.5
  54.4 1.3 collective-permute-start
  55.7 1.3 collective-permute-start.1
  57.1 21.0 %collective-permute-done.4 = bf16[1,2,128,512]{3,2,1,0:T(8,128)(2,1)S(1)} collective-permute-done((bf16[1,2,128,512]{3,2,1,0:T(8,128)(2,1)S(1)}, bf16[1,2,128,512]{3,2,1,0:T(8,128)(2,1)S(1)}, u32[]{:S(2)}, u32[]{:S(2)}) %collective-permute-start.4) | collective-permute-done | bytes 262176 | tf_op jit(solution)/shard_map/ppermute | solution.py:15
  78.2 1.9 collective-permute-start.6
  80.2 3.9 %collective-permute-start.7 = (bf16[3,1,128,512]{3,2,1,0:T(8,128)(2,1)S(1)}, bf16[3,1,128,512]{3,2,1,0:T(8,128)(2,1)S(1)}, u32[]{:S(2)}, u32[]{:S(2)}) collective-permute-start(bf16[3,1,128,512]{3,2,1,0:T(8,128)(2,1)S(1)} %get-tuple-element.24), channel_id=1, source_target_pairs={{1,0},{2,1},{3,2},{4,3},{5,4},{6,5},{7,6},{9,8},{10,9},{11,10},{12... | collective-permute-start | bytes 1179656 | tf_op jit(solution)/shard_map/ppermute | solution.py:26
  84.1 6.9 %collective-permute-done.1 = bf16[1,2,128,512]{3,2,1,0:T(8,128)(2,1)S(1)} collective-permute-done((bf16[1,2,128,512]{3,2,1,0:T(8,128)(2,1)S(1)}, bf16[1,2,128,512]{3,2,1,0:T(8,128)(2,1)S(1)}, u32[]{:S(2)}, u32[]{:S(2)}) %collective-permute-start.1) | collective-permute-done | bytes 262176 | tf_op jit(solution)/shard_map/ppermute | solution.py:15
  91.1 1.9 collective-permute-start.2
  93.0 3.9 %collective-permute-start.3 = (bf16[3,1,128,512]{3,2,1,0:T(8,128)(2,1)S(1)}, bf16[3,1,128,512]{3,2,1,0:T(8,128)(2,1)S(1)}, u32[]{:S(2)}, u32[]{:S(2)}) collective-permute-start(bf16[3,1,128,512]{3,2,1,0:T(8,128)(2,1)S(1)} %get-tuple-element.26), channel_id=1, source_target_pairs={{1,0},{2,1},{3,2},{4,3},{5,4},{6,5},{7,6},{9,8},{10,9},{11,10},{12... | collective-permute-start | bytes 1179656 | tf_op jit(solution)/shard_map/ppermute | solution.py:26
  97.0 2.8 %collective-permute-done.7 = bf16[3,1,128,512]{3,2,1,0:T(8,128)(2,1)S(1)} collective-permute-done((bf16[3,1,128,512]{3,2,1,0:T(8,128)(2,1)S(1)}, bf16[3,1,128,512]{3,2,1,0:T(8,128)(2,1)S(1)}, u32[]{:S(2)}, u32[]{:S(2)}) %collective-permute-start.7) | collective-permute-done | bytes 393248 | tf_op jit(solution)/shard_map/ppermute | solution.py:26
  101.8 6.5 %collective-permute-done.3 = bf16[3,1,128,512]{3,2,1,0:T(8,128)(2,1)S(1)} collective-permute-done((bf16[3,1,128,512]{3,2,1,0:T(8,128)(2,1)S(1)}, bf16[3,1,128,512]{3,2,1,0:T(8,128)(2,1)S(1)}, u32[]{:S(2)}, u32[]{:S(2)}) %collective-permute-start.3) | collective-permute-done | bytes 393248 | tf_op jit(solution)/shard_map/ppermute | solution.py:26
  111.3 1.1 copy-done.6
  120.1 4.7 %convolution_bitcast_fusion.4 = f32[256,512]{1,0:T(8,128)} fusion(bf16[256,9,512]{2,0,1:T(8,128)(2,1)S(1)} %constant_dynamic-update-slice_fusion.12, bf16[9,512,512]{2,1,0:T(8,128)(2,1)} %all-gather.8.cloned.1.call-done), kind=kOutput, calls=%fused_computation.14 | convolution fusion | flops 1207959552 | bytes 7602176 | tf_op jit(solution)/shard_map/dot_general | solution.py:94
  124.8 1.4 convolution_bitcast_fusion.5
  126.2 29.5 %all-gather.6.cloned.1.call-done = bf16[9,512,512]{2,1,0:T(8,128)(2,1)} async-done(((bf16[9,16,512]{2,1,0:T(8,128)(2,1)}), bf16[9,512,512]{2,1,0:T(8,128)(2,1)}) %all-gather.6.cloned.1.call-update) | async-done | bytes 4718608 | tf_op jit(solution)/shard_map/all_gather | solution.py:56
  155.6 5.5 %fusion.3 = f32[256,512]{1,0:T(8,128)} fusion(f32[256,512]{1,0:T(8,128)} %convolution_bitcast_fusion.4, bf16[256,9,512]{2,0,1:T(8,128)(2,1)} %copy-done.7, bf16[9,512,512]{2,1,0:T(8,128)(2,1)} %all-gather.6.cloned.1.call-done), kind=kOutput, calls=%fused_computation.17 | convolution fusion | flops 1208090624 | bytes 8126464 | tf_op jit(solution)/shard_map/dot_general | solution.py:94
  161.1 2.2 fusion.2
  163.3 55.1 %all-gather.4.cloned.1.call-done = bf16[9,512,512]{2,1,0:T(8,128)(2,1)} async-done(((bf16[9,16,512]{2,1,0:T(8,128)(2,1)}), bf16[9,512,512]{2,1,0:T(8,128)(2,1)}) %all-gather.4.cloned.1.call-update) | async-done | bytes 4718608 | tf_op jit(solution)/shard_map/all_gather | solution.py:56
  218.4 4.5 %fusion.5 = f32[256,512]{1,0:T(8,128)S(1)} fusion(f32[256,512]{1,0:T(8,128)} %fusion.2, bf16[256,9,512]{2,0,1:T(8,128)(2,1)} %constant_dynamic-update-slice_fusion.48, bf16[9,512,512]{2,1,0:T(8,128)(2,1)} %all-gather.4.cloned.1.call-done), kind=kOutput, calls=%fused_computation.19 | convolution fusion | flops 1208090624 | bytes 8126464 | tf_op jit(solution)/shard_map/dot_general | solution.py:89
  224.7 2.1 collective-permute-start.11
  227.8 1.2 collective-permute-start.13
  229.7 3.3 %collective-permute-start.8 = (f32[2,1,32]{2,1,0:T(1,128)S(1)}, f32[2,1,32]{2,1,0:T(1,128)S(1)}, u32[]{:S(2)}, u32[]{:S(2)}) collective-permute-start(f32[2,1,32]{2,1,0:T(1,128)S(1)} %pad_maximum_fusion.1), channel_id=1, source_target_pairs={{0,1},{1,2},{2,3},{3,4},{4,5},{5,6},{6,7},{7,0},{8,9},{9,10},{10,1... | collective-permute-start | bytes 776 | tf_op jit(solution)/shard_map/ppermute | solution.py:110
  233.1 1.2 collective-permute-start.9
  234.2 4.4 %fusion.4 = f32[256,512]{1,0:T(8,128)S(1)} fusion(f32[256,512]{1,0:T(8,128)S(1)} %copy-done.11, bf16[256,9,512]{2,0,1:T(8,128)(2,1)} %constant_dynamic-update-slice_fusion.39, bf16[9,512,512]{2,1,0:T(8,128)(2,1)} %all-gather.4.cloned.1.call-done), kind=kOutput, calls=%fused_computation.18 | convolution fusion | flops 1208090624 | bytes 8126464 | tf_op jit(solution)/shard_map/dot_general | solution.py:94
  239.1 1.1 fusion.24
  (134 shorter events, 17.9 us)
Async XLA Ops:
  7.2 47.3 %copy-start.1 = (bf16[1,2,128,512]{3,2,1,0:T(8,128)(2,1)S(1)}, bf16[1,2,128,512]{3,2,1,0:T(8,128)(2,1)}, u32[]{:S(2)}) copy-start(bf16[1,2,128,512]{3,2,1,0:T(8,128)(2,1)} %param.7) | copy-start | bytes 786436
  7.2 112.9 %all-gather.8.cloned.1.call-start = ((), (), s32[]{:S(2)}) async-start(), calls=%async_computation.2 | async-start | bytes 4866048 | tf_op jit(solution)/shard_map/all_gather | solution.py:56
  9.1 146.5 %all-gather.6.cloned.1.call-start = ((), (), s32[]{:S(2)}) async-start(), calls=%async_computation.1 | async-start | bytes 4866048 | tf_op jit(solution)/shard_map/all_gather | solution.py:56
  9.8 208.6 %all-gather.4.cloned.1.call-start = ((), (), s32[]{:S(2)}) async-start(), calls=%async_computation | async-start | bytes 4866048 | tf_op jit(solution)/shard_map/all_gather | solution.py:56
  47.8 30.3 %collective-permute-start.4 = (bf16[1,2,128,512]{3,2,1,0:T(8,128)(2,1)S(1)}, bf16[1,2,128,512]{3,2,1,0:T(8,128)(2,1)S(1)}, u32[]{:S(2)}, u32[]{:S(2)}) collective-permute-start(bf16[1,2,128,512]{3,2,1,0:T(8,128)(2,1)S(1)} %fusion.17), channel_id=1, source_target_pairs={{0,16},{8,24},{16,32},{24,40},{32,48},{40,56},{48,64},{56,72},{64,... | collective-permute-start | bytes 786440 | tf_op jit(solution)/shard_map/ppermute | solution.py:15
  53.1 24.9 %collective-permute-start.5 = (bf16[1,2,128,512]{3,2,1,0:T(8,128)(2,1)S(1)}, bf16[1,2,128,512]{3,2,1,0:T(8,128)(2,1)S(1)}, u32[]{:S(2)}, u32[]{:S(2)}) collective-permute-start(bf16[1,2,128,512]{3,2,1,0:T(8,128)(2,1)S(1)} %fusion.17), channel_id=1, source_target_pairs={{0,8},{8,16},{16,24},{24,32},{32,40},{40,48},{48,56},{56,64},{64,7... | collective-permute-start | bytes 786440 | tf_op jit(solution)/shard_map/ppermute | solution.py:15
  54.4 29.7 %collective-permute-start = (bf16[1,2,128,512]{3,2,1,0:T(8,128)(2,1)S(1)}, bf16[1,2,128,512]{3,2,1,0:T(8,128)(2,1)S(1)}, u32[]{:S(2)}, u32[]{:S(2)}) collective-permute-start(bf16[1,2,128,512]{3,2,1,0:T(8,128)(2,1)S(1)} %copy-done.1), channel_id=1, source_target_pairs={{8,0},{16,8},{24,16},{32,24},{40,32},{48,40},{56,48},{64,56},{72,6... | collective-permute-start | bytes 786440 | tf_op jit(solution)/shard_map/ppermute | solution.py:15
  55.7 35.3 %collective-permute-start.1 = (bf16[1,2,128,512]{3,2,1,0:T(8,128)(2,1)S(1)}, bf16[1,2,128,512]{3,2,1,0:T(8,128)(2,1)S(1)}, u32[]{:S(2)}, u32[]{:S(2)}) collective-permute-start(bf16[1,2,128,512]{3,2,1,0:T(8,128)(2,1)S(1)} %copy-done.1), channel_id=1, source_target_pairs={{16,0},{24,8},{32,16},{40,24},{48,32},{56,40},{64,48},{72,56},{80,... | collective-permute-start | bytes 786440 | tf_op jit(solution)/shard_map/ppermute | solution.py:15
  78.2 18.8 %collective-permute-start.6 = (bf16[3,1,128,512]{3,2,1,0:T(8,128)(2,1)S(1)}, bf16[3,1,128,512]{3,2,1,0:T(8,128)(2,1)S(1)}, u32[]{:S(2)}, u32[]{:S(2)}) collective-permute-start(bf16[3,1,128,512]{3,2,1,0:T(8,128)(2,1)S(1)} %get-tuple-element.23), channel_id=1, source_target_pairs={{0,1},{1,2},{2,3},{3,4},{4,5},{5,6},{6,7},{8,9},{9,10},{10,11},{11... | collective-permute-start | bytes 1179656 | tf_op jit(solution)/shard_map/ppermute | solution.py:25
  80.2 19.6 %collective-permute-start.7 = (bf16[3,1,128,512]{3,2,1,0:T(8,128)(2,1)S(1)}, bf16[3,1,128,512]{3,2,1,0:T(8,128)(2,1)S(1)}, u32[]{:S(2)}, u32[]{:S(2)}) collective-permute-start(bf16[3,1,128,512]{3,2,1,0:T(8,128)(2,1)S(1)} %get-tuple-element.24), channel_id=1, source_target_pairs={{1,0},{2,1},{3,2},{4,3},{5,4},{6,5},{7,6},{9,8},{10,9},{11,10},{12... | collective-permute-start | bytes 1179656 | tf_op jit(solution)/shard_map/ppermute | solution.py:26
  91.1 10.6 %collective-permute-start.2 = (bf16[3,1,128,512]{3,2,1,0:T(8,128)(2,1)S(1)}, bf16[3,1,128,512]{3,2,1,0:T(8,128)(2,1)S(1)}, u32[]{:S(2)}, u32[]{:S(2)}) collective-permute-start(bf16[3,1,128,512]{3,2,1,0:T(8,128)(2,1)S(1)} %get-tuple-element.25), channel_id=1, source_target_pairs={{0,1},{1,2},{2,3},{3,4},{4,5},{5,6},{6,7},{8,9},{9,10},{10,11},{11... | collective-permute-start | bytes 1179656 | tf_op jit(solution)/shard_map/ppermute | solution.py:25
  93.0 15.2 %collective-permute-start.3 = (bf16[3,1,128,512]{3,2,1,0:T(8,128)(2,1)S(1)}, bf16[3,1,128,512]{3,2,1,0:T(8,128)(2,1)S(1)}, u32[]{:S(2)}, u32[]{:S(2)}) collective-permute-start(bf16[3,1,128,512]{3,2,1,0:T(8,128)(2,1)S(1)} %get-tuple-element.26), channel_id=1, source_target_pairs={{1,0},{2,1},{3,2},{4,3},{5,4},{6,5},{7,6},{9,8},{10,9},{11,10},{12... | collective-permute-start | bytes 1179656 | tf_op jit(solution)/shard_map/ppermute | solution.py:26
  111.0 1.4 copy-start.6
  111.2 1.9 copy-start.7
  113.3 1.5 copy-start.4
  113.6 5.8 %copy-start.2 = (bf16[256,9,512]{2,0,1:T(8,128)(2,1)}, bf16[256,9,512]{2,0,1:T(8,128)(2,1)S(1)}, u32[]{:S(2)}) copy-start(bf16[256,9,512]{2,0,1:T(8,128)(2,1)S(1)} %constant_dynamic-update-slice_fusion.21) | copy-start | bytes 7077892
  120.1 4.7 %copy-start.5 = (bf16[256,9,512]{2,0,1:T(8,128)(2,1)S(1)}, bf16[256,9,512]{2,0,1:T(8,128)(2,1)}, u32[]{:S(2)}) copy-start(bf16[256,9,512]{2,0,1:T(8,128)(2,1)} %copy-done.4) | copy-start | bytes 7077892
  120.1 4.7 %copy-start.9 = (bf16[9,512,512]{2,1,0:T(8,128)(2,1)S(1)}, bf16[9,512,512]{2,1,0:T(8,128)(2,1)}, u32[]{:S(2)}) copy-start(bf16[9,512,512]{2,1,0:T(8,128)(2,1)} %all-gather.8.cloned.1.call-done) | copy-start | bytes 14155780
  155.6 5.5 %copy-start.3 = (bf16[256,9,512]{2,0,1:T(8,128)(2,1)S(1)}, bf16[256,9,512]{2,0,1:T(8,128)(2,1)}, u32[]{:S(2)}) copy-start(bf16[256,9,512]{2,0,1:T(8,128)(2,1)} %copy-done.2) | copy-start | bytes 7077892
  155.6 5.5 %copy-start.10 = (bf16[9,512,512]{2,1,0:T(8,128)(2,1)S(1)}, bf16[9,512,512]{2,1,0:T(8,128)(2,1)}, u32[]{:S(2)}) copy-start(bf16[9,512,512]{2,1,0:T(8,128)(2,1)} %all-gather.6.cloned.1.call-done) | copy-start | bytes 14155780
  163.3 59.6 %copy-start = (bf16[1,2,128,512]{3,2,1,0:T(8,128)(2,1)S(1)}, bf16[1,2,128,512]{3,2,1,0:T(8,128)(2,1)}, u32[]{:S(2)}) copy-start(bf16[1,2,128,512]{3,2,1,0:T(8,128)(2,1)} %param.4) | copy-start | bytes 786436
  163.3 59.6 %copy-start.8 = (f32[512]{0:T(512)S(1)}, f32[512]{0:T(512)}, u32[]{:S(2)}) copy-start(f32[512]{0:T(512)} %param.5) | copy-start | bytes 6148
  163.3 70.9 %copy-start.11 = (f32[256,512]{1,0:T(8,128)S(1)}, f32[256,512]{1,0:T(8,128)}, u32[]{:S(2)}) copy-start(f32[256,512]{1,0:T(8,128)} %fusion.3) | copy-start | bytes 1572868
  223.7 6.0 %collective-permute-start.10 = (f32[2,1,32]{2,1,0:T(1,128)S(1)}, f32[2,1,32]{2,1,0:T(1,128)S(1)}, u32[]{:S(2)}, u32[]{:S(2)}) collective-permute-start(f32[2,1,32]{2,1,0:T(1,128)S(1)} %pad_maximum_fusion.1), channel_id=1, source_target_pairs={{0,3},{1,4},{2,5},{3,6},{4,7},{5,0},{6,1},{7,2},{8,11},{9,12},{10,... | collective-permute-start | bytes 776 | tf_op jit(solution)/shard_map/ppermute | solution.py:110
  224.7 8.4 %collective-permute-start.11 = (f32[2,1,32]{2,1,0:T(1,128)S(1)}, f32[2,1,32]{2,1,0:T(1,128)S(1)}, u32[]{:S(2)}, u32[]{:S(2)}) collective-permute-start(f32[2,1,32]{2,1,0:T(1,128)S(1)} %pad_maximum_fusion.1), channel_id=1, source_target_pairs={{0,4},{1,5},{2,6},{3,7},{4,0},{5,1},{6,2},{7,3},{8,12},{9,13},{10,... | collective-permute-start | bytes 776 | tf_op jit(solution)/shard_map/ppermute | solution.py:110
  226.8 11.8 %collective-permute-start.12 = (f32[2,1,32]{2,1,0:T(1,128)S(1)}, f32[2,1,32]{2,1,0:T(1,128)S(1)}, u32[]{:S(2)}, u32[]{:S(2)}) collective-permute-start(f32[2,1,32]{2,1,0:T(1,128)S(1)} %pad_maximum_fusion.1), channel_id=1, source_target_pairs={{0,5},{1,6},{2,7},{3,0},{4,1},{5,2},{6,3},{7,4},{8,13},{9,14},{10,... | collective-permute-start | bytes 776 | tf_op jit(solution)/shard_map/ppermute | solution.py:110
  227.8 10.9 %collective-permute-start.13 = (f32[2,1,32]{2,1,0:T(1,128)S(1)}, f32[2,1,32]{2,1,0:T(1,128)S(1)}, u32[]{:S(2)}, u32[]{:S(2)}) collective-permute-start(f32[2,1,32]{2,1,0:T(1,128)S(1)} %pad_maximum_fusion.1), channel_id=1, source_target_pairs={{0,6},{1,7},{2,0},{3,1},{4,2},{5,3},{6,4},{7,5},{8,14},{9,15},{10,... | collective-permute-start | bytes 776 | tf_op jit(solution)/shard_map/ppermute | solution.py:110
  228.9 9.8 %collective-permute-start.14 = (f32[2,1,32]{2,1,0:T(1,128)S(1)}, f32[2,1,32]{2,1,0:T(1,128)S(1)}, u32[]{:S(2)}, u32[]{:S(2)}) collective-permute-start(f32[2,1,32]{2,1,0:T(1,128)S(1)} %pad_maximum_fusion.1), channel_id=1, source_target_pairs={{0,7},{1,0},{2,1},{3,2},{4,3},{5,4},{6,5},{7,6},{8,15},{9,8},{10,9... | collective-permute-start | bytes 776 | tf_op jit(solution)/shard_map/ppermute | solution.py:110
  229.7 9.0 %collective-permute-start.8 = (f32[2,1,32]{2,1,0:T(1,128)S(1)}, f32[2,1,32]{2,1,0:T(1,128)S(1)}, u32[]{:S(2)}, u32[]{:S(2)}) collective-permute-start(f32[2,1,32]{2,1,0:T(1,128)S(1)} %pad_maximum_fusion.1), channel_id=1, source_target_pairs={{0,1},{1,2},{2,3},{3,4},{4,5},{5,6},{6,7},{7,0},{8,9},{9,10},{10,1... | collective-permute-start | bytes 776 | tf_op jit(solution)/shard_map/ppermute | solution.py:110
  233.1 5.6 %collective-permute-start.9 = (f32[2,1,32]{2,1,0:T(1,128)S(1)}, f32[2,1,32]{2,1,0:T(1,128)S(1)}, u32[]{:S(2)}, u32[]{:S(2)}) collective-permute-start(f32[2,1,32]{2,1,0:T(1,128)S(1)} %pad_maximum_fusion.1), channel_id=1, source_target_pairs={{0,2},{1,3},{2,4},{3,5},{4,6},{5,7},{6,0},{7,1},{8,10},{9,11},{10,... | collective-permute-start | bytes 776 | tf_op jit(solution)/shard_map/ppermute | solution.py:110
Sparse Core Ops, SparseCore 0:
  11.2 77.4 all-gather.7
  91.4 64.2 all-gather.5
  158.3 60.0 all-gather.3
